TPU v7x, 32 devices: a whole 2x2x4 slice. The times are simulated.
32 devices in a mesh: groups: 2 (over y), inner: 16 (over z, x, core).
Axes of the slice: x: 2, y: 2, z: 4, core: 2. Of those that a mesh axis runs over, the one named last changes fastest.
Arguments:
- ticks: bfloat16 [262144, 128], P(('groups', 'inner')), parts along dimension 0, may hold values from -6 to 6
- conv_weight: bfloat16 [2048, 768], replicated, may hold values from -0.125 to 0.125
- norm_gain: float32 [768], replicated, may hold values from 0.25 to 1.75
- qkv_weight: bfloat16 [768, 2304], replicated, may hold values from -0.21875 to 0.21875
- head_gain: float32 [768], replicated, may hold values from 0.25 to 1.75
- out_weight: bfloat16 [768, 768], replicated, may hold values from -0.21875 to 0.21875
- state_in: float32 [24, 64, 64], P('groups'), parts along dimension 0, may hold values from -768 to 768
Outputs:
- layer_out: bfloat16 [32768, 768], P(('groups', 'inner')), parts along dimension 0
There are 2 independent parts, one for each index of `groups`. A program takes and returns all parts, laid end to end along the dimension named above; an argument that names none is the same for every part. Nothing has to cross between parts.
All inputs are finite; a program needn't handle non-finite values.
Results may differ from a plain program's by a relative error of at most 0.008.
Values may be sent and summed in bfloat16 or wider, within the bound.
No kernel may reach another device: no remote copies, remote signals or barrier semaphores. Data moves between devices by JAX's collectives and lax.ppermute only.
A program may use at most 192 MiB of HBM per device.

v0:
```python
import jax
import jax.numpy as jnp
from jax import lax
from jax.sharding import PartitionSpec as P

STRIDE = 8
BLK = 512


def from_behind(value, axis, steps):
    count = lax.axis_size(axis)
    initial, last = (max(0, -steps), min(count, count - steps))
    return lax.ppermute(value, axis, [(source, source + steps) for source in range(initial, last)])


def shards(ticks, conv_weight, norm_gain, qkv_weight, head_gain, out_weight, state_in):
    row_width = STRIDE * ticks.shape[1]
    token_count = ticks.shape[0] // STRIDE
    tick_rows = ticks.reshape(token_count, row_width)
    weight_prev = conv_weight[:row_width]
    current = jnp.dot(tick_rows, conv_weight[row_width:], preferred_element_type=jnp.float32)
    last_row = from_behind(tick_rows[token_count - 1 :], "inner", 1)
    earlier_rows = jnp.concatenate([last_row, tick_rows[:-1]], 0)
    embedded_f = current + jnp.dot(earlier_rows, weight_prev, preferred_element_type=jnp.float32)
    embedded = embedded_f.astype(jnp.bfloat16)
    embed_f = embedded.astype(jnp.float32)
    normed = (
        embed_f * lax.rsqrt(jnp.mean(embed_f * embed_f, -1, keepdims=True) + 1e-05) * norm_gain
    ).astype(jnp.bfloat16)
    qkv = jnp.dot(normed, qkv_weight, preferred_element_type=jnp.float32).astype(jnp.bfloat16)
    model_width = embedded.shape[1]
    head_count = state_in.shape[0]
    head_size = state_in.shape[1]
    block_count = token_count // BLK
    queries = qkv[:, :model_width].reshape(block_count, BLK, head_count, head_size)
    keys_all = qkv[:, model_width : 2 * model_width].reshape(
        block_count, BLK, head_count, head_size
    )
    values_all = qkv[:, 2 * model_width :].reshape(block_count, BLK, head_count, head_size)
    block_states = jnp.einsum(
        "bthi,bthj->bhij", keys_all, values_all, preferred_element_type=jnp.float32
    )
    local_state = jnp.sum(block_states, 0)
    every_state = lax.all_gather(local_state[None], "inner", axis=0, tiled=True)
    lower_dev = (jnp.arange(every_state.shape[0]) < lax.axis_index("inner")).astype(jnp.float32)
    prefix = jnp.einsum("n,nhij->hij", lower_dev, every_state, precision=lax.Precision.HIGHEST)
    carried = state_in + prefix
    within = jnp.cumsum(block_states, 0) - block_states
    state_before = carried[None] + within
    lower = jnp.arange(BLK)[:, None] >= jnp.arange(BLK)[None, :]
    scores = jnp.einsum("bthd,bshd->bhts", queries, keys_all, preferred_element_type=jnp.float32)
    scores = jnp.where(lower[None, None], scores, 0.0).astype(jnp.bfloat16)
    inside_term = jnp.einsum(
        "bhts,bshd->bthd", scores, values_all, preferred_element_type=jnp.float32
    )
    carried_term = jnp.einsum(
        "bthi,bhij->bthj",
        queries.astype(jnp.float32),
        state_before,
        precision=lax.Precision.HIGHEST,
    )
    combined = (inside_term + carried_term).reshape(token_count, head_count, head_size)
    attended = (
        combined
        * lax.rsqrt(jnp.mean(combined * combined, -1, keepdims=True) + 1e-06)
        * head_gain.reshape(head_count, head_size)
    )
    attended = attended.reshape(token_count, model_width).astype(jnp.bfloat16)
    return (embed_f + jnp.dot(attended, out_weight, preferred_element_type=jnp.float32)).astype(
        jnp.bfloat16
    )


def solution(mesh):
    in_specs = (P(("groups", "inner"), None), P(), P(), P(), P(), P(), P("groups", None, None))
    out_specs = P(("groups", "inner"), None)
    return jax.shard_map(shards, mesh=mesh, in_specs=in_specs, out_specs=out_specs, check_vma=False)
```

profile of v0, /device:TPU:0, one launch (start us, length us, event | category | flops | bytes accessed | tf_op | source)
XLA Modules:
  0.0 145.3 jit_solution(13970756868127508273)
XLA Ops:
  6.5 0.8 slice_bitcast_fusion
  7.4 2.5 %collective-permute-start = (bf16[1,1024]{1,0:T(2,128)(2,1)S(1)}, bf16[1,1024]{1,0:T(2,128)(2,1)S(1)}, u32[]{:S(2)}, u32[]{:S(2)}) collective-permute-start(bf16[1,1024]{1,0:T(2,128)(2,1)S(1)} %bitcast.53), channel_id=1, source_target_pairs={{0,1},{1,2},{2,3},{3,4},{4,5},{5,6},{6,7},{7,8},{8,9},{9,10},{10,1... | collective-permute-start | bytes 6152 | tf_op jit(solution)/shard_map/ppermute | solution.py:13
  9.9 4.2 %reshape.62 = bf16[1024,1024]{1,0:T(8,128)(2,1)} reshape(bf16[8192,128]{1,0:T(8,128)(2,1)} %param.7) | data formatting | bytes 4194304 | tf_op jit(solution)/shard_map/reshape | solution.py:19
  14.0 5.7 %fusion.21 = f32[1024,768]{0,1:T(8,128)} fusion(bf16[1024,1024]{1,0:T(8,128)(2,1)} %reshape.62, bf16[2048,768]{1,0:T(8,128)(2,1)} %param.8), kind=kOutput, calls=%fused_computation.28 | convolution fusion | flops 1610612736 | bytes 6815744 | tf_op jit(solution)/shard_map/dot_general | solution.py:21
  19.7 1.5 %slice.30 = bf16[8184,128]{1,0:T(8,128)(2,1)} slice(bf16[8192,128]{1,0:T(8,128)(2,1)S(1)} %copy-done.2), slice={[0:8184], [0:128]} | slice | bytes 4190208 | tf_op jit(solution)/shard_map/slice | solution.py:23
  21.2 4.2 %slice.31 = bf16[1023,1024]{1,0:T(8,128)(2,1)} reshape(bf16[8184,128]{1,0:T(8,128)(2,1)} %slice.30) | data formatting | bytes 4190208 | tf_op jit(solution)/shard_map/slice | solution.py:23
  25.3 5.0 %fusion.7 = (f32[1024]{0:T(1024)S(1)}, bf16[1024,768]{0,1:T(8,128)(2,1)S(1)}) fusion(f32[1024,768]{0,1:T(8,128)} %fusion.21, bf16[2048,768]{1,0:T(8,128)(2,1)} %param.8, bf16[1023,1024]{1,0:T(8,128)(2,1)} %slice.31, bf16[1,1024]{1,0:T(2,128)(2,1)S(1)} %collective-permute-done), kind=kOutput, calls=%fused_computation.11 | convolution fusion | flops 1618738176 | bytes 8394752 | tf_op jit(solution)/shard_map/dot_general | solution.py:24
  30.4 4.4 %convolution_convert_fusion = bf16[1024,2304]{1,0:T(8,128)(2,1)S(1)} fusion(bf16[768,2304]{1,0:T(8,128)(2,1)S(1)} %copy-done, bf16[1024,768]{0,1:T(8,128)(2,1)S(1)} %get-tuple-element.9, f32[768]{0:T(1024)S(1)} %copy-done.11, f32[1024]{0:T(1024)S(1)} %add_rsqrt_fusion.1), kind=kOutput, calls=%fused_computation.7 | convolution fusion | flops 3629383680 | bytes 9837568 | tf_op jit(solution)/shard_map/dot_general | solution.py:30
  34.8 1.5 %fusion.43 = (bf16[1024,768]{1,0:T(8,128)(2,1)S(1)}, bf16[1024,768]{1,0:T(8,128)(2,1)S(1)}, bf16[1024,768]{1,0:T(8,128)(2,1)}) fusion(bf16[1024,2304]{1,0:T(8,128)(2,1)S(1)} %convolution_convert_fusion), kind=kLoop, calls=%fused_computation.51 | loop fusion | bytes 9437184 | tf_op jit(solution)/shard_map/slice | solution.py:35
  36.2 2.6 %copy.39 = bf16[1024,768]{0,1:T(8,128)(2,1)} copy(bf16[1024,768]{1,0:T(8,128)(2,1)} %get-tuple-element.7) | data formatting | bytes 3145728 | tf_op jit(solution)/shard_map/slice | solution.py:39
  38.8 3.9 %reshape.63 = bf16[2,512,12,64]{1,0,3,2:T(2,128)(2,1)} reshape(bf16[1024,768]{0,1:T(8,128)(2,1)} %copy.39) | data formatting | bytes 3145728 | tf_op jit(solution)/shard_map/reshape | solution.py:39
  42.7 1.7 %copy.41 = bf16[1024,768]{0,1:T(8,128)(2,1)} copy(bf16[1024,768]{1,0:T(8,128)(2,1)S(1)} %get-tuple-element.6) | data formatting | bytes 3145728 | tf_op jit(solution)/shard_map/slice | solution.py:36
  44.4 4.0 %reshape.65 = bf16[2,512,12,64]{1,0,3,2:T(2,128)(2,1)} reshape(bf16[1024,768]{0,1:T(8,128)(2,1)} %copy.41) | data formatting | bytes 3145728 | tf_op jit(solution)/shard_map/reshape | solution.py:36
  48.3 3.7 %fusion.44 = (f32[12,64,64]{2,1,0:T(8,128)}, f32[2,12,64,64]{3,2,1,0:T(8,128)}) fusion(bf16[2,512,12,64]{1,0,3,2:T(2,128)(2,1)S(1)} %copy-done.7, bf16[2,512,12,64]{1,0,3,2:T(2,128)(2,1)} %reshape.65), kind=kOutput, calls=%fused_computation.52 | convolution fusion | flops 100712448 | bytes 3735552 | tf_op jit(solution)/shard_map/bthi,bthj->bhij/dot_general | solution.py:40
  52.0 0.0 all-gather.3.cloned.1.call-update
  52.0 0.1 iota_compare_fusion
  52.1 0.8 copy.40
  52.9 1.2 reshape.64
  54.1 10.5 %fusion = f32[2,12,64,512]{3,2,1,0:T(8,128)} fusion(pred[512,512]{1,0:T(8,128)(4,1)S(1)} %iota_compare_fusion, bf16[2,512,12,64]{1,0,3,2:T(2,128)(2,1)} %reshape.63, bf16[2,512,12,64]{1,0,3,2:T(2,128)(2,1)} %reshape.65, bf16[2,512,12,64]{1,0,3,2:T(2,128)(2,1)S(1)} %reshape.64), kind=kOutput, calls=%fused_computation.1 | convolution fusion | flops 1623195648 | bytes 8126464 | tf_op jit(solution)/shard_map/bhts,bshd->bthd/dot_general | solution.py:53
  64.6 52.0 %all-gather.3.cloned.1.call-done = f32[192,64,64]{2,1,0:T(8,128)} async-done(((f32[12,64,64]{2,1,0:T(8,128)}), f32[192,64,64]{2,1,0:T(8,128)}) %all-gather.3.cloned.1.call-update) | async-done | bytes 3145744 | tf_op jit(solution)/shard_map/all_gather | solution.py:44
  116.6 8.4 %fusion.5 = f32[1,12,64,64]{3,0,2,1:T(1,128)S(1)} fusion(f32[16,12,64,64]{3,2,1,0:T(8,128)} %bitcast.48, s32[]{:T(128)S(6)} %axis_index.12), kind=kOutput, calls=%fused_computation.5 | convolution fusion | flops 9437200 | bytes 3342340 | tf_op jit(solution)/shard_map/n,nhij->hij/dot_general | solution.py:46
  125.1 0.5 fusion.27
  125.6 0.8 copy-done.4
  126.4 1.7 %multiply_reduce_fusion = (f32[2,512,12]{1,2,0:T(8,128)S(1)}, f32[2,512,12,64]{1,3,2,0:T(8,128)S(1)}) fusion(f32[2,12,64,512]{3,2,1,0:T(8,128)S(1)} %copy-done.5, f32[2,12,64,64]{3,2,1,0:T(8,128)S(1)} %fusion.27, bf16[2,512,12,64]{1,0,3,2:T(2,128)(2,1)S(1)} %copy-done.4), kind=kOutput, calls=%fused_computation.18 | convolution fusion | flops 606326784 | bytes 8306688 | tf_op jit(solution)/shard_map/bthi,bhij->bthj/dot_general | solution.py:56
  128.2 2.4 %copy.49 = f32[2,512,12,64]{1,0,3,2:T(2,128)S(1)} copy(f32[2,512,12,64]{1,3,2,0:T(8,128)S(1)} %get-tuple-element.13) | data formatting | bytes 6291456 | tf_op jit(solution)/shard_map/add | solution.py:62
  130.6 0.7 copy.59
  131.5 0.0 copy-start.10
  131.5 0.4 fusion.12
  131.9 0.9 copy-done.10
  132.8 0.5 copy-done.13
  133.3 2.6 %fusion.10 = bf16[1024,768]{0,1:T(8,128)(2,1)} fusion(bf16[1024,768]{0,1:T(8,128)(2,1)S(1)} %copy-done.13, bf16[1024,768]{0,1:T(8,128)(2,1)S(1)} %fusion.12, bf16[768,768]{1,0:T(8,128)(2,1)S(1)} %copy-done.10), kind=kOutput, calls=%fused_computation.14 | convolution fusion | flops 1210318848 | bytes 5898240 | tf_op jit(solution)/shard_map/dot_general | solution.py:69
  135.9 2.6 %copy.52 = bf16[1024,768]{1,0:T(8,128)(2,1)} copy(bf16[1024,768]{0,1:T(8,128)(2,1)} %fusion.10) | data formatting | bytes 3145728 | tf_op jit(solution)/shard_map/convert_element_type | solution.py:69
  (33 shorter events, 0.2 us)
Async XLA Ops:
  6.5 23.8 %copy-start = (bf16[768,2304]{1,0:T(8,128)(2,1)S(1)}, bf16[768,2304]{1,0:T(8,128)(2,1)}, u32[]{:S(2)}) copy-start(bf16[768,2304]{1,0:T(8,128)(2,1)} %param.10) | copy-start | bytes 10616836
  6.5 110.0 %all-gather.3.cloned.1.call-start = ((), (), s32[]{:S(2)}) async-start(), calls=%async_computation | async-start | bytes 6684672 | tf_op jit(solution)/shard_map/all_gather | solution.py:44
  7.4 18.0 %collective-permute-start = (bf16[1,1024]{1,0:T(2,128)(2,1)S(1)}, bf16[1,1024]{1,0:T(2,128)(2,1)S(1)}, u32[]{:S(2)}, u32[]{:S(2)}) collective-permute-start(bf16[1,1024]{1,0:T(2,128)(2,1)S(1)} %bitcast.53), channel_id=1, source_target_pairs={{0,1},{1,2},{2,3},{3,4},{4,5},{5,6},{6,7},{7,8},{8,9},{9,10},{10,1... | collective-permute-start | bytes 6152 | tf_op jit(solution)/shard_map/ppermute | solution.py:13
  14.0 5.7 %copy-start.2 = (bf16[8192,128]{1,0:T(8,128)(2,1)S(1)}, bf16[8192,128]{1,0:T(8,128)(2,1)}, u32[]{:S(2)}) copy-start(bf16[8192,128]{1,0:T(8,128)(2,1)} %param.7) | copy-start | bytes 6291460
  25.3 5.0 %copy-start.11 = (f32[768]{0:T(1024)S(1)}, f32[768]{0:T(1024)}, u32[]{:S(2)}) copy-start(f32[768]{0:T(1024)} %param.9) | copy-start | bytes 9220
  30.3 4.4 %copy-start.12 = (bf16[1024,768]{0,1:T(8,128)(2,1)}, bf16[1024,768]{0,1:T(8,128)(2,1)S(1)}, u32[]{:S(2)}) copy-start(bf16[1024,768]{0,1:T(8,128)(2,1)S(1)} %get-tuple-element.9) | copy-start | bytes 4718596
  44.4 4.0 %copy-start.7 = (bf16[2,512,12,64]{1,0,3,2:T(2,128)(2,1)S(1)}, bf16[2,512,12,64]{1,0,3,2:T(2,128)(2,1)}, u32[]{:S(2)}) copy-start(bf16[2,512,12,64]{1,0,3,2:T(2,128)(2,1)} %reshape.63) | copy-start | bytes 4718596
  54.1 10.5 %copy-start.3 = (bf16[2,512,12,64]{1,0,3,2:T(2,128)(2,1)}, bf16[2,512,12,64]{1,0,3,2:T(2,128)(2,1)S(1)}, u32[]{:S(2)}) copy-start(bf16[2,512,12,64]{1,0,3,2:T(2,128)(2,1)S(1)} %reshape.64) | copy-start | bytes 4718596
  116.6 8.5 %copy-start.8 = (f32[12,64,64]{2,1,0:T(8,128)S(1)}, f32[12,64,64]{2,1,0:T(8,128)}, u32[]{:S(2)}) copy-start(f32[12,64,64]{2,1,0:T(8,128)} %param.13) | copy-start | bytes 589828
  116.6 8.5 %copy-start.6 = (f32[2,12,64,64]{3,2,1,0:T(8,128)S(1)}, f32[2,12,64,64]{3,2,1,0:T(8,128)}, u32[]{:S(2)}) copy-start(f32[2,12,64,64]{3,2,1,0:T(8,128)} %get-tuple-element.11) | copy-start | bytes 1179652
  116.6 9.0 %copy-start.5 = (f32[2,12,64,512]{3,2,1,0:T(8,128)S(1)}, f32[2,12,64,512]{3,2,1,0:T(8,128)}, u32[]{:S(2)}) copy-start(f32[2,12,64,512]{3,2,1,0:T(8,128)} %fusion) | copy-start | bytes 9437188
  125.0 1.4 copy-start.4
  130.6 0.9 copy-start.9
  131.5 1.3 copy-start.10
  131.5 1.8 %copy-start.13 = (bf16[1024,768]{0,1:T(8,128)(2,1)S(1)}, bf16[1024,768]{0,1:T(8,128)(2,1)}, u32[]{:S(2)}) copy-start(bf16[1024,768]{0,1:T(8,128)(2,1)} %copy-done.12) | copy-start | bytes 4718596
  133.3 5.2 %copy-start.1 = (bf16[768,2304]{1,0:T(8,128)(2,1)S(1)}, bf16[768,2304]{1,0:T(8,128)(2,1)}, u32[]{:S(2)}) copy-start(bf16[768,2304]{1,0:T(8,128)(2,1)} %param.10) | copy-start | bytes 10616836
Sparse Core Ops, SparseCore 0:
  52.1 64.4 all-gather.2
where the time goes:
time: 146 us; the launch traced here: 145 us
  waiting for transfers between devices  52 us (36%)
  matrix products  42 us (29%)
  local copies, waits for them, and re-layouts  34.2 us (23%)
  between operations  13.7 us (9%)
  starting transfers between devices  2.48 us (2%)
    all_gather x1, waiting for transfers between devices, shards(): every_state = lax.all_gather(local_state[None], 'inner', axis=0, tiled=True)  52 us
    dot_general x1, matrix products, shards(): jnp.einsum('bhts,bshd->bthd', scores, values_all, preferred_element_type=...  10.5 us
    dot_general x1, matrix products, shards(): jnp.einsum('n,nhij->hij', lower_dev, every_state, precision=lax.Precision...  8.42 us
    dot_general x1, matrix products, shards(): jnp.dot(tick_rows, conv_weight[row_width:], preferred_element_type=jnp.fl...  5.66 us
    slice x2, local copies, waits for them, and re-layouts, shards(): earlier_rows = jnp.concatenate([last_row, tick_rows[:-1]], 0)  5.64 us
    dot_general x1, matrix products, shards(): jnp.dot(earlier_rows, weight_prev, preferred_element_type=jnp.float32)  4.97 us
    dot_general x1, matrix products, shards(): jnp.dot(normed, qkv_weight, preferred_element_type=jnp.float32)  4.36 us
    reshape x1, local copies, waits for them, and re-layouts, shards(): tick_rows = ticks.reshape(token_count, row_width)  4.17 us
  transfers between devices with their start and end apart: 2, of which 1 were waited for; matrix products, arithmetic and copies ran while one was open for 19% of the time, Pallas kernels for 0%

commit v1 on v0

--- a/solution.py
+++ b/solution.py
@@ -41,7 +41,14 @@
         "bthi,bthj->bhij", keys_all, values_all, preferred_element_type=jnp.float32
     )
     local_state = jnp.sum(block_states, 0)
-    every_state = lax.all_gather(local_state[None], "inner", axis=0, tiled=True)
+    ring = [local_state[None]]
+    for hop in range(15):
+        ring.append(lax.ppermute(ring[-1], "inner", [(dev, (dev + 1) % 16) for dev in range(16)]))
+    every_state = jnp.roll(
+        jnp.concatenate(ring[::-1], axis=0),
+        (lax.axis_index("inner") + 1) * ring[0].shape[0],
+        axis=0,
+    )
     lower_dev = (jnp.arange(every_state.shape[0]) < lax.axis_index("inner")).astype(jnp.float32)
     prefix = jnp.einsum("n,nhij->hij", lower_dev, every_state, precision=lax.Precision.HIGHEST)
     carried = state_in + prefix

time: 146 us -> 233 us (1.60)
  waiting for transfers between devices: 52 us -> 134 us
  local copies, waits for them, and re-layouts: 34.2 us -> 51.5 us
  between operations: 13.7 us -> 0.73 us
  matrix products: 42 us -> 38.9 us
  starting transfers between devices: 2.48 us -> 5.12 us
    ppermute x0 -> x15, waiting for transfers between devices: none -> 134 us  [shards(): lax.ppermute(ring[-1], 'inner', [(dev, (dev + 1) % 16) for dev in range(1...]
    all_gather x1 -> x0, waiting for transfers between devices: 52 us -> none  [shards(): every_state = lax.all_gather(local_state[None], 'inner', axis=0, tiled=True)]
    unnamed x33 -> x112, local copies, waits for them, and re-layouts: 3.83 us -> 21.1 us
    ppermute x0 -> x15, starting transfers between devices: none -> 2.65 us  [shards(): lax.ppermute(ring[-1], 'inner', [(dev, (dev + 1) % 16) for dev in range(1...]
    dot_general x1, matrix products: 8.42 us -> 5.99 us  [shards(): jnp.einsum('n,nhij->hij', lower_dev, every_state, precision=lax.Precision...]
  transfers between devices with their start and end apart: 2 -> 16, of which waited for: 1 -> 15; matrix products, arithmetic and copies ran while one was open for 19% -> 12% of each run, Pallas kernels for 0% -> 0%
where the time goes in v1:
time: 233 us; the launch traced here: 232 us
  waiting for transfers between devices  134 us (58%)
  local copies, waits for them, and re-layouts  51.5 us (22%)
  matrix products  38.9 us (17%)
  starting transfers between devices  5.12 us (2%)
    ppermute x15, waiting for transfers between devices, shards(): lax.ppermute(ring[-1], 'inner', [(dev, (dev + 1) % 16) for dev in range(1...  134 us
    unnamed x112, local copies, waits for them, and re-layouts  21.1 us
    dot_general x1, matrix products, shards(): jnp.einsum('bhts,bshd->bthd', scores, values_all, preferred_element_type=...  9.97 us
    dot_general x1, matrix products, shards(): jnp.einsum('n,nhij->hij', lower_dev, every_state, precision=lax.Precision...  5.99 us
    dot_general x1, matrix products, shards(): jnp.dot(tick_rows, conv_weight[row_width:], preferred_element_type=jnp.fl...  5.68 us
    slice x2, local copies, waits for them, and re-layouts, shards(): earlier_rows = jnp.concatenate([last_row, tick_rows[:-1]], 0)  5.64 us
    dot_general x1, matrix products, shards(): jnp.dot(earlier_rows, weight_prev, preferred_element_type=jnp.float32)  4.96 us
  transfers between devices with their start and end apart: 16, of which 15 were waited for; matrix products, arithmetic and copies ran while one was open for 12% of the time, Pallas kernels for 0%

profile of v1, /device:TPU:0, one launch (start us, length us, event | category | flops | bytes accessed | tf_op | source)
XLA Modules:
  0.0 231.8 jit_solution(15967008535976070781)
XLA Ops:
  0.8 2.5 %collective-permute-start = (bf16[1,1024]{1,0:T(2,128)(2,1)S(1)}, bf16[1,1024]{1,0:T(2,128)(2,1)S(1)}, u32[]{:S(2)}, u32[]{:S(2)}) collective-permute-start(bf16[1,1024]{1,0:T(2,128)(2,1)S(1)} %bitcast.55), channel_id=1, source_target_pairs={{0,1},{1,2},{2,3},{3,4},{4,5},{5,6},{6,7},{7,8},{8,9},{9,10},{10,1... | collective-permute-start | bytes 6152 | tf_op jit(solution)/shard_map/ppermute | solution.py:13
  3.3 4.2 %reshape.62 = bf16[1024,1024]{1,0:T(8,128)(2,1)} reshape(bf16[8192,128]{1,0:T(8,128)(2,1)} %param.7) | data formatting | bytes 4194304 | tf_op jit(solution)/shard_map/reshape | solution.py:19
  7.5 5.7 %fusion.21 = f32[1024,768]{0,1:T(8,128)} fusion(bf16[1024,1024]{1,0:T(8,128)(2,1)} %reshape.62, bf16[2048,768]{1,0:T(8,128)(2,1)} %param.8), kind=kOutput, calls=%fused_computation.28 | convolution fusion | flops 1610612736 | bytes 6815744 | tf_op jit(solution)/shard_map/dot_general | solution.py:21
  14.7 4.2 %slice.31 = bf16[1023,1024]{1,0:T(8,128)(2,1)} reshape(bf16[8184,128]{1,0:T(8,128)(2,1)} %slice.30) | data formatting | bytes 4190208 | tf_op jit(solution)/shard_map/slice | solution.py:23
  18.9 5.0 %fusion.7 = (f32[1024]{0:T(1024)S(1)}, bf16[1024,768]{0,1:T(8,128)(2,1)S(1)}) fusion(f32[1024,768]{0,1:T(8,128)} %fusion.21, bf16[2048,768]{1,0:T(8,128)(2,1)} %param.8, bf16[1023,1024]{1,0:T(8,128)(2,1)} %slice.31, bf16[1,1024]{1,0:T(2,128)(2,1)S(1)} %collective-permute-done), kind=kOutput, calls=%fused_computation.11 | convolution fusion | flops 1618738176 | bytes 8394752 | tf_op jit(solution)/shard_map/dot_general | solution.py:24
  23.9 4.4 %convolution_convert_fusion = bf16[1024,2304]{1,0:T(8,128)(2,1)S(1)} fusion(bf16[768,2304]{1,0:T(8,128)(2,1)S(1)} %copy-done, bf16[1024,768]{0,1:T(8,128)(2,1)S(1)} %get-tuple-element.9, f32[768]{0:T(1024)S(1)} %copy-done.35, f32[1024]{0:T(1024)S(1)} %add_rsqrt_fusion.1), kind=kOutput, calls=%fused_computation.7 | convolution fusion | flops 3629383680 | bytes 9837568 | tf_op jit(solution)/shard_map/dot_general | solution.py:30
  29.7 2.6 %copy.39 = bf16[1024,768]{0,1:T(8,128)(2,1)} copy(bf16[1024,768]{1,0:T(8,128)(2,1)} %get-tuple-element.7) | data formatting | bytes 3145728 | tf_op jit(solution)/shard_map/slice | solution.py:39
  32.3 3.8 %reshape.63 = bf16[2,512,12,64]{1,0,3,2:T(2,128)(2,1)} reshape(bf16[1024,768]{0,1:T(8,128)(2,1)} %copy.39) | data formatting | bytes 3145728 | tf_op jit(solution)/shard_map/reshape | solution.py:39
  36.2 1.6 copy.41
  37.8 2.9 %reshape.65 = bf16[2,512,12,64]{1,0,3,2:T(2,128)(2,1)S(1)} reshape(bf16[1024,768]{0,1:T(8,128)(2,1)} %copy.41) | data formatting | bytes 3145728 | tf_op jit(solution)/shard_map/reshape | solution.py:36
  40.7 3.5 %fusion.44 = (f32[12,64,64]{2,1,0:T(8,128)S(1)}, f32[2,12,64,64]{3,2,1,0:T(8,128)}) fusion(bf16[2,512,12,64]{1,0,3,2:T(2,128)(2,1)} %reshape.63, bf16[2,512,12,64]{1,0,3,2:T(2,128)(2,1)S(1)} %reshape.65), kind=kOutput, calls=%fused_computation.85 | convolution fusion | flops 100712448 | bytes 3735552 | tf_op jit(solution)/shard_map/bthi,bthj->bhij/dot_general | solution.py:40
  44.2 2.6 %collective-permute-start.1 = (f32[1,12,64,64]{3,2,1,0:T(8,128)S(1)}, f32[1,12,64,64]{3,2,1,0:T(8,128)S(1)}, u32[]{:S(2)}, u32[]{:S(2)}) collective-permute-start(f32[1,12,64,64]{3,2,1,0:T(8,128)S(1)} %bitcast.50), channel_id=1, source_target_pairs={{0,1},{1,2},{2,3},{3,4},{4,5},{5,6},{6,7},{7,8},{8,9},{9,10},{10,1... | collective-permute-start | bytes 589832 | tf_op jit(solution)/shard_map/ppermute | solution.py:46
  46.8 7.3 %collective-permute-done.1 = f32[1,12,64,64]{3,2,1,0:T(8,128)S(1)} collective-permute-done((f32[1,12,64,64]{3,2,1,0:T(8,128)S(1)}, f32[1,12,64,64]{3,2,1,0:T(8,128)S(1)}, u32[]{:S(2)}, u32[]{:S(2)}) %collective-permute-start.1) | collective-permute-done | bytes 196640 | tf_op jit(solution)/shard_map/ppermute | solution.py:46
  54.9 9.9 %collective-permute-done.2 = f32[1,12,64,64]{3,2,1,0:T(8,128)S(1)} collective-permute-done((f32[1,12,64,64]{3,2,1,0:T(8,128)S(1)}, f32[1,12,64,64]{3,2,1,0:T(8,128)S(1)}, u32[]{:S(2)}, u32[]{:S(2)}) %collective-permute-start.2) | collective-permute-done | bytes 196640 | tf_op jit(solution)/shard_map/ppermute | solution.py:46
  65.5 9.9 %collective-permute-done.3 = f32[1,12,64,64]{3,2,1,0:T(8,128)S(1)} collective-permute-done((f32[1,12,64,64]{3,2,1,0:T(8,128)S(1)}, f32[1,12,64,64]{3,2,1,0:T(8,128)S(1)}, u32[]{:S(2)}, u32[]{:S(2)}) %collective-permute-start.3) | collective-permute-done | bytes 196640 | tf_op jit(solution)/shard_map/ppermute | solution.py:46
  76.2 9.9 %collective-permute-done.4 = f32[1,12,64,64]{3,2,1,0:T(8,128)S(1)} collective-permute-done((f32[1,12,64,64]{3,2,1,0:T(8,128)S(1)}, f32[1,12,64,64]{3,2,1,0:T(8,128)S(1)}, u32[]{:S(2)}, u32[]{:S(2)}) %collective-permute-start.4) | collective-permute-done | bytes 196640 | tf_op jit(solution)/shard_map/ppermute | solution.py:46
  86.8 9.9 %collective-permute-done.5 = f32[1,12,64,64]{3,2,1,0:T(8,128)S(1)} collective-permute-done((f32[1,12,64,64]{3,2,1,0:T(8,128)S(1)}, f32[1,12,64,64]{3,2,1,0:T(8,128)S(1)}, u32[]{:S(2)}, u32[]{:S(2)}) %collective-permute-start.5) | collective-permute-done | bytes 196640 | tf_op jit(solution)/shard_map/ppermute | solution.py:46
  97.5 9.9 %collective-permute-done.6 = f32[1,12,64,64]{3,2,1,0:T(8,128)S(1)} collective-permute-done((f32[1,12,64,64]{3,2,1,0:T(8,128)S(1)}, f32[1,12,64,64]{3,2,1,0:T(8,128)S(1)}, u32[]{:S(2)}, u32[]{:S(2)}) %collective-permute-start.6) | collective-permute-done | bytes 196640 | tf_op jit(solution)/shard_map/ppermute | solution.py:46
  108.1 9.9 %collective-permute-done.7 = f32[1,12,64,64]{3,2,1,0:T(8,128)S(1)} collective-permute-done((f32[1,12,64,64]{3,2,1,0:T(8,128)S(1)}, f32[1,12,64,64]{3,2,1,0:T(8,128)S(1)}, u32[]{:S(2)}, u32[]{:S(2)}) %collective-permute-start.7) | collective-permute-done | bytes 196640 | tf_op jit(solution)/shard_map/ppermute | solution.py:46
  118.8 9.9 %collective-permute-done.8 = f32[1,12,64,64]{3,2,1,0:T(8,128)S(1)} collective-permute-done((f32[1,12,64,64]{3,2,1,0:T(8,128)S(1)}, f32[1,12,64,64]{3,2,1,0:T(8,128)S(1)}, u32[]{:S(2)}, u32[]{:S(2)}) %collective-permute-start.8) | collective-permute-done | bytes 196640 | tf_op jit(solution)/shard_map/ppermute | solution.py:46
  129.4 9.9 %collective-permute-done.9 = f32[1,12,64,64]{3,2,1,0:T(8,128)S(1)} collective-permute-done((f32[1,12,64,64]{3,2,1,0:T(8,128)S(1)}, f32[1,12,64,64]{3,2,1,0:T(8,128)S(1)}, u32[]{:S(2)}, u32[]{:S(2)}) %collective-permute-start.9) | collective-permute-done | bytes 196640 | tf_op jit(solution)/shard_map/ppermute | solution.py:46
  140.1 9.9 %collective-permute-done.10 = f32[1,12,64,64]{3,2,1,0:T(8,128)S(1)} collective-permute-done((f32[1,12,64,64]{3,2,1,0:T(8,128)S(1)}, f32[1,12,64,64]{3,2,1,0:T(8,128)S(1)}, u32[]{:S(2)}, u32[]{:S(2)}) %collective-permute-start.10) | collective-permute-done | bytes 196640 | tf_op jit(solution)/shard_map/ppermute | solution.py:46
  150.7 9.9 %collective-permute-done.11 = f32[1,12,64,64]{3,2,1,0:T(8,128)S(1)} collective-permute-done((f32[1,12,64,64]{3,2,1,0:T(8,128)S(1)}, f32[1,12,64,64]{3,2,1,0:T(8,128)S(1)}, u32[]{:S(2)}, u32[]{:S(2)}) %collective-permute-start.11) | collective-permute-done | bytes 196640 | tf_op jit(solution)/shard_map/ppermute | solution.py:46
  161.4 9.9 %collective-permute-done.12 = f32[1,12,64,64]{3,2,1,0:T(8,128)S(1)} collective-permute-done((f32[1,12,64,64]{3,2,1,0:T(8,128)S(1)}, f32[1,12,64,64]{3,2,1,0:T(8,128)S(1)}, u32[]{:S(2)}, u32[]{:S(2)}) %collective-permute-start.12) | collective-permute-done | bytes 196640 | tf_op jit(solution)/shard_map/ppermute | solution.py:46
  172.1 10.0 %collective-permute-done.13 = f32[1,12,64,64]{3,2,1,0:T(8,128)} collective-permute-done((f32[1,12,64,64]{3,2,1,0:T(8,128)S(1)}, f32[1,12,64,64]{3,2,1,0:T(8,128)}, u32[]{:S(2)}, u32[]{:S(2)}) %collective-permute-start.13) | collective-permute-done | bytes 196640 | tf_op jit(solution)/shard_map/ppermute | solution.py:46
  184.8 7.5 %collective-permute-done.14 = f32[1,12,64,64]{3,2,1,0:T(8,128)} collective-permute-done((f32[1,12,64,64]{3,2,1,0:T(8,128)}, f32[1,12,64,64]{3,2,1,0:T(8,128)}, u32[]{:S(2)}, u32[]{:S(2)}) %collective-permute-start.14) | collective-permute-done | bytes 196640 | tf_op jit(solution)/shard_map/ppermute | solution.py:46
  192.3 10.0 %fusion = f32[2,12,64,512]{3,2,1,0:T(8,128)} fusion(pred[512,512]{1,0:T(8,128)(4,1)} %iota_compare_fusion, bf16[2,512,12,64]{1,0,3,2:T(2,128)(2,1)} %reshape.63, bf16[2,512,12,64]{1,0,3,2:T(2,128)(2,1)} %copy-done.7, bf16[2,512,12,64]{1,0,3,2:T(2,128)(2,1)S(1)} %reshape.64), kind=kOutput, calls=%fused_computation.1 | convolution fusion | flops 1623195648 | bytes 8126464 | tf_op jit(solution)/shard_map/bhts,bshd->bthd/dot_general | solution.py:60
  213.2 6.0 %fusion.5 = f32[1,12,64,64]{3,0,2,1:T(1,128)S(1)} fusion(f32[16,12,64,64]{3,2,1,0:T(8,128)S(1)} %constant_dynamic-slice_fusion, s32[]{:T(128)S(6)} %axis_index.16), kind=kOutput, calls=%fused_computation.5 | convolution fusion | flops 9437200 | bytes 3342340 | tf_op jit(solution)/shard_map/n,nhij->hij/dot_general | solution.py:53
  219.8 1.7 multiply_reduce_fusion
  221.6 2.4 %copy.49 = f32[2,512,12,64]{1,0,3,2:T(2,128)S(1)} copy(f32[2,512,12,64]{1,3,2,0:T(8,128)S(1)} %get-tuple-element.13) | data formatting | bytes 6291456 | tf_op jit(solution)/shard_map/add | solution.py:69
  226.6 2.7 %fusion.10 = bf16[1024,768]{0,1:T(8,128)(2,1)} fusion(bf16[1024,768]{0,1:T(8,128)(2,1)S(1)} %copy-done.37, bf16[1024,768]{0,1:T(8,128)(2,1)S(1)} %fusion.12, bf16[768,768]{1,0:T(8,128)(2,1)S(1)} %copy-done.34), kind=kOutput, calls=%fused_computation.14 | convolution fusion | flops 1210318848 | bytes 5898240 | tf_op jit(solution)/shard_map/dot_general | solution.py:76
  229.2 2.6 %copy.52 = bf16[1024,768]{1,0:T(8,128)(2,1)} copy(bf16[1024,768]{0,1:T(8,128)(2,1)} %fusion.10) | data formatting | bytes 3145728 | tf_op jit(solution)/shard_map/convert_element_type | solution.py:76
  (141 shorter events, 29.1 us)
Async XLA Ops:
  0.0 23.8 %copy-start = (bf16[768,2304]{1,0:T(8,128)(2,1)S(1)}, bf16[768,2304]{1,0:T(8,128)(2,1)}, u32[]{:S(2)}) copy-start(bf16[768,2304]{1,0:T(8,128)(2,1)} %param.10) | copy-start | bytes 10616836
  0.8 18.0 %collective-permute-start = (bf16[1,1024]{1,0:T(2,128)(2,1)S(1)}, bf16[1,1024]{1,0:T(2,128)(2,1)S(1)}, u32[]{:S(2)}, u32[]{:S(2)}) collective-permute-start(bf16[1,1024]{1,0:T(2,128)(2,1)S(1)} %bitcast.55), channel_id=1, source_target_pairs={{0,1},{1,2},{2,3},{3,4},{4,5},{5,6},{6,7},{7,8},{8,9},{9,10},{10,1... | collective-permute-start | bytes 6152 | tf_op jit(solution)/shard_map/ppermute | solution.py:13
  7.5 5.7 %copy-start.2 = (bf16[8192,128]{1,0:T(8,128)(2,1)S(1)}, bf16[8192,128]{1,0:T(8,128)(2,1)}, u32[]{:S(2)}) copy-start(bf16[8192,128]{1,0:T(8,128)(2,1)} %param.7) | copy-start | bytes 6291460
  40.7 142.2 %copy-start.7 = (bf16[2,512,12,64]{1,0,3,2:T(2,128)(2,1)}, bf16[2,512,12,64]{1,0,3,2:T(2,128)(2,1)S(1)}, u32[]{:S(2)}) copy-start(bf16[2,512,12,64]{1,0,3,2:T(2,128)(2,1)S(1)} %reshape.65) | copy-start | bytes 4718596
  44.2 9.9 %collective-permute-start.1 = (f32[1,12,64,64]{3,2,1,0:T(8,128)S(1)}, f32[1,12,64,64]{3,2,1,0:T(8,128)S(1)}, u32[]{:S(2)}, u32[]{:S(2)}) collective-permute-start(f32[1,12,64,64]{3,2,1,0:T(8,128)S(1)} %bitcast.50), channel_id=1, source_target_pairs={{0,1},{1,2},{2,3},{3,4},{4,5},{5,6},{6,7},{7,8},{8,9},{9,10},{10,1... | collective-permute-start | bytes 589832 | tf_op jit(solution)/shard_map/ppermute | solution.py:46
  54.9 9.9 %collective-permute-start.2 = (f32[1,12,64,64]{3,2,1,0:T(8,128)S(1)}, f32[1,12,64,64]{3,2,1,0:T(8,128)S(1)}, u32[]{:S(2)}, u32[]{:S(2)}) collective-permute-start(f32[1,12,64,64]{3,2,1,0:T(8,128)S(1)} %collective-permute-done.1), channel_id=1, source_target_pairs={{0,1},{1,2},{2,3},{3,4},{4,5},{5,6},{6,7},{7,8},{8,9},{9,10},{10,1... | collective-permute-start | bytes 589832 | tf_op jit(solution)/shard_map/ppermute | solution.py:46
  65.5 9.9 %collective-permute-start.3 = (f32[1,12,64,64]{3,2,1,0:T(8,128)S(1)}, f32[1,12,64,64]{3,2,1,0:T(8,128)S(1)}, u32[]{:S(2)}, u32[]{:S(2)}) collective-permute-start(f32[1,12,64,64]{3,2,1,0:T(8,128)S(1)} %collective-permute-done.2), channel_id=1, source_target_pairs={{0,1},{1,2},{2,3},{3,4},{4,5},{5,6},{6,7},{7,8},{8,9},{9,10},{10,1... | collective-permute-start | bytes 589832 | tf_op jit(solution)/shard_map/ppermute | solution.py:46
  76.2 9.9 %collective-permute-start.4 = (f32[1,12,64,64]{3,2,1,0:T(8,128)S(1)}, f32[1,12,64,64]{3,2,1,0:T(8,128)S(1)}, u32[]{:S(2)}, u32[]{:S(2)}) collective-permute-start(f32[1,12,64,64]{3,2,1,0:T(8,128)S(1)} %collective-permute-done.3), channel_id=1, source_target_pairs={{0,1},{1,2},{2,3},{3,4},{4,5},{5,6},{6,7},{7,8},{8,9},{9,10},{10,1... | collective-permute-start | bytes 589832 | tf_op jit(solution)/shard_map/ppermute | solution.py:46
  86.8 9.9 %collective-permute-start.5 = (f32[1,12,64,64]{3,2,1,0:T(8,128)S(1)}, f32[1,12,64,64]{3,2,1,0:T(8,128)S(1)}, u32[]{:S(2)}, u32[]{:S(2)}) collective-permute-start(f32[1,12,64,64]{3,2,1,0:T(8,128)S(1)} %collective-permute-done.4), channel_id=1, source_target_pairs={{0,1},{1,2},{2,3},{3,4},{4,5},{5,6},{6,7},{7,8},{8,9},{9,10},{10,1... | collective-permute-start | bytes 589832 | tf_op jit(solution)/shard_map/ppermute | solution.py:46
  97.5 9.9 %collective-permute-start.6 = (f32[1,12,64,64]{3,2,1,0:T(8,128)S(1)}, f32[1,12,64,64]{3,2,1,0:T(8,128)S(1)}, u32[]{:S(2)}, u32[]{:S(2)}) collective-permute-start(f32[1,12,64,64]{3,2,1,0:T(8,128)S(1)} %collective-permute-done.5), channel_id=1, source_target_pairs={{0,1},{1,2},{2,3},{3,4},{4,5},{5,6},{6,7},{7,8},{8,9},{9,10},{10,1... | collective-permute-start | bytes 589832 | tf_op jit(solution)/shard_map/ppermute | solution.py:46
  108.1 9.9 %collective-permute-start.7 = (f32[1,12,64,64]{3,2,1,0:T(8,128)S(1)}, f32[1,12,64,64]{3,2,1,0:T(8,128)S(1)}, u32[]{:S(2)}, u32[]{:S(2)}) collective-permute-start(f32[1,12,64,64]{3,2,1,0:T(8,128)S(1)} %collective-permute-done.6), channel_id=1, source_target_pairs={{0,1},{1,2},{2,3},{3,4},{4,5},{5,6},{6,7},{7,8},{8,9},{9,10},{10,1... | collective-permute-start | bytes 589832 | tf_op jit(solution)/shard_map/ppermute | solution.py:46
  118.8 9.9 %collective-permute-start.8 = (f32[1,12,64,64]{3,2,1,0:T(8,128)S(1)}, f32[1,12,64,64]{3,2,1,0:T(8,128)S(1)}, u32[]{:S(2)}, u32[]{:S(2)}) collective-permute-start(f32[1,12,64,64]{3,2,1,0:T(8,128)S(1)} %collective-permute-done.7), channel_id=1, source_target_pairs={{0,1},{1,2},{2,3},{3,4},{4,5},{5,6},{6,7},{7,8},{8,9},{9,10},{10,1... | collective-permute-start | bytes 589832 | tf_op jit(solution)/shard_map/ppermute | solution.py:46
  129.4 9.9 %collective-permute-start.9 = (f32[1,12,64,64]{3,2,1,0:T(8,128)S(1)}, f32[1,12,64,64]{3,2,1,0:T(8,128)S(1)}, u32[]{:S(2)}, u32[]{:S(2)}) collective-permute-start(f32[1,12,64,64]{3,2,1,0:T(8,128)S(1)} %collective-permute-done.8), channel_id=1, source_target_pairs={{0,1},{1,2},{2,3},{3,4},{4,5},{5,6},{6,7},{7,8},{8,9},{9,10},{10,1... | collective-permute-start | bytes 589832 | tf_op jit(solution)/shard_map/ppermute | solution.py:46
  140.1 9.9 %collective-permute-start.10 = (f32[1,12,64,64]{3,2,1,0:T(8,128)S(1)}, f32[1,12,64,64]{3,2,1,0:T(8,128)S(1)}, u32[]{:S(2)}, u32[]{:S(2)}) collective-permute-start(f32[1,12,64,64]{3,2,1,0:T(8,128)S(1)} %collective-permute-done.9), channel_id=1, source_target_pairs={{0,1},{1,2},{2,3},{3,4},{4,5},{5,6},{6,7},{7,8},{8,9},{9,10},{10,1... | collective-permute-start | bytes 589832 | tf_op jit(solution)/shard_map/ppermute | solution.py:46
  150.7 9.9 %collective-permute-start.11 = (f32[1,12,64,64]{3,2,1,0:T(8,128)S(1)}, f32[1,12,64,64]{3,2,1,0:T(8,128)S(1)}, u32[]{:S(2)}, u32[]{:S(2)}) collective-permute-start(f32[1,12,64,64]{3,2,1,0:T(8,128)S(1)} %collective-permute-done.10), channel_id=1, source_target_pairs={{0,1},{1,2},{2,3},{3,4},{4,5},{5,6},{6,7},{7,8},{8,9},{9,10},{10,1... | collective-permute-start | bytes 589832 | tf_op jit(solution)/shard_map/ppermute | solution.py:46
  161.4 9.9 %collective-permute-start.12 = (f32[1,12,64,64]{3,2,1,0:T(8,128)S(1)}, f32[1,12,64,64]{3,2,1,0:T(8,128)S(1)}, u32[]{:S(2)}, u32[]{:S(2)}) collective-permute-start(f32[1,12,64,64]{3,2,1,0:T(8,128)S(1)} %collective-permute-done.11), channel_id=1, source_target_pairs={{0,1},{1,2},{2,3},{3,4},{4,5},{5,6},{6,7},{7,8},{8,9},{9,10},{10,1... | collective-permute-start | bytes 589832 | tf_op jit(solution)/shard_map/ppermute | solution.py:46
  172.1 10.0 %collective-permute-start.13 = (f32[1,12,64,64]{3,2,1,0:T(8,128)S(1)}, f32[1,12,64,64]{3,2,1,0:T(8,128)}, u32[]{:S(2)}, u32[]{:S(2)}) collective-permute-start(f32[1,12,64,64]{3,2,1,0:T(8,128)S(1)} %collective-permute-done.12), channel_id=1, source_target_pairs={{0,1},{1,2},{2,3},{3,4},{4,5},{5,6},{6,7},{7,8},{8,9},{9,10},{10,1... | collective-permute-start | bytes 589832 | tf_op jit(solution)/shard_map/ppermute | solution.py:46
  182.1 10.2 %collective-permute-start.14 = (f32[1,12,64,64]{3,2,1,0:T(8,128)}, f32[1,12,64,64]{3,2,1,0:T(8,128)}, u32[]{:S(2)}, u32[]{:S(2)}) collective-permute-start(f32[1,12,64,64]{3,2,1,0:T(8,128)} %collective-permute-done.13), channel_id=1, source_target_pairs={{0,1},{1,2},{2,3},{3,4},{4,5},{5,6},{6,7},{7,8},{8,9},{9,10},{10,1... | collective-permute-start | bytes 589832 | tf_op jit(solution)/shard_map/ppermute | solution.py:46
  184.8 17.5 %copy-start.3 = (bf16[2,512,12,64]{1,0,3,2:T(2,128)(2,1)}, bf16[2,512,12,64]{1,0,3,2:T(2,128)(2,1)S(1)}, u32[]{:S(2)}) copy-start(bf16[2,512,12,64]{1,0,3,2:T(2,128)(2,1)S(1)} %reshape.64) | copy-start | bytes 4718596
  192.3 10.2 %collective-permute-start.15 = (f32[1,12,64,64]{3,2,1,0:T(8,128)}, f32[1,12,64,64]{3,2,1,0:T(8,128)}, u32[]{:S(2)}, u32[]{:S(2)}) collective-permute-start(f32[1,12,64,64]{3,2,1,0:T(8,128)} %collective-permute-done.14), channel_id=1, source_target_pairs={{0,1},{1,2},{2,3},{3,4},{4,5},{5,6},{6,7},{7,8},{8,9},{9,10},{10,1... | collective-permute-start | bytes 589832 | tf_op jit(solution)/shard_map/ppermute | solution.py:46
  202.3 5.7 %copy-start.27 = (f32[1,12,64,64]{3,2,1,0:T(8,128)S(1)}, f32[1,12,64,64]{3,2,1,0:T(8,128)}, u32[]{:S(2)}) copy-start(f32[1,12,64,64]{3,2,1,0:T(8,128)} %copy-done.26) | copy-start | bytes 589828
  202.3 5.7 %copy-start.25 = (f32[1,12,64,64]{3,2,1,0:T(8,128)S(1)}, f32[1,12,64,64]{3,2,1,0:T(8,128)}, u32[]{:S(2)}) copy-start(f32[1,12,64,64]{3,2,1,0:T(8,128)} %copy-done.24) | copy-start | bytes 589828
  202.3 5.8 %copy-start.23 = (f32[1,12,64,64]{3,2,1,0:T(8,128)S(1)}, f32[1,12,64,64]{3,2,1,0:T(8,128)}, u32[]{:S(2)}) copy-start(f32[1,12,64,64]{3,2,1,0:T(8,128)} %copy-done.22) | copy-start | bytes 589828
  202.3 5.8 %copy-start.21 = (f32[1,12,64,64]{3,2,1,0:T(8,128)S(1)}, f32[1,12,64,64]{3,2,1,0:T(8,128)}, u32[]{:S(2)}) copy-start(f32[1,12,64,64]{3,2,1,0:T(8,128)} %copy-done.20) | copy-start | bytes 589828
  202.3 5.9 %copy-start.19 = (f32[1,12,64,64]{3,2,1,0:T(8,128)S(1)}, f32[1,12,64,64]{3,2,1,0:T(8,128)}, u32[]{:S(2)}) copy-start(f32[1,12,64,64]{3,2,1,0:T(8,128)} %copy-done.18) | copy-start | bytes 589828
  202.3 5.9 %copy-start.17 = (f32[1,12,64,64]{3,2,1,0:T(8,128)S(1)}, f32[1,12,64,64]{3,2,1,0:T(8,128)}, u32[]{:S(2)}) copy-start(f32[1,12,64,64]{3,2,1,0:T(8,128)} %copy-done.16) | copy-start | bytes 589828
  202.3 5.9 %copy-start.15 = (f32[1,12,64,64]{3,2,1,0:T(8,128)S(1)}, f32[1,12,64,64]{3,2,1,0:T(8,128)}, u32[]{:S(2)}) copy-start(f32[1,12,64,64]{3,2,1,0:T(8,128)} %copy-done.14) | copy-start | bytes 589828
  213.2 6.0 %copy-start.32 = (f32[12,64,64]{2,1,0:T(8,128)S(1)}, f32[12,64,64]{2,1,0:T(8,128)}, u32[]{:S(2)}) copy-start(f32[12,64,64]{2,1,0:T(8,128)} %param.13) | copy-start | bytes 589828
  213.2 6.1 %copy-start.6 = (f32[2,12,64,64]{3,2,1,0:T(8,128)S(1)}, f32[2,12,64,64]{3,2,1,0:T(8,128)}, u32[]{:S(2)}) copy-start(f32[2,12,64,64]{3,2,1,0:T(8,128)} %get-tuple-element.11) | copy-start | bytes 1179652
  213.2 6.6 %copy-start.4 = (bf16[2,512,12,64]{1,0,3,2:T(2,128)(2,1)S(1)}, bf16[2,512,12,64]{1,0,3,2:T(2,128)(2,1)}, u32[]{:S(2)}) copy-start(bf16[2,512,12,64]{1,0,3,2:T(2,128)(2,1)} %copy-done.3) | copy-start | bytes 4718596
  213.2 6.6 %copy-start.5 = (f32[2,12,64,512]{3,2,1,0:T(8,128)S(1)}, f32[2,12,64,512]{3,2,1,0:T(8,128)}, u32[]{:S(2)}) copy-start(f32[2,12,64,512]{3,2,1,0:T(8,128)} %fusion) | copy-start | bytes 9437188
  226.6 5.3 %copy-start.1 = (bf16[768,2304]{1,0:T(8,128)(2,1)S(1)}, bf16[768,2304]{1,0:T(8,128)(2,1)}, u32[]{:S(2)}) copy-start(bf16[768,2304]{1,0:T(8,128)(2,1)} %param.10) | copy-start | bytes 10616836
  (22 other events, 40.1 us)
